TPU v7x, 128 devices: a whole 4x4x4 slice. The times are simulated.
128 devices in a mesh: section: 8 (over y, core), seq: 16 (over z, x).
Axes of the slice: x: 4, y: 4, z: 4, core: 2. Of those that a mesh axis runs over, the one named last changes fastest.
Arguments:
- hidden: bfloat16 [2, 2048, 4096], P(None, 'seq'), may hold values from -6 to 6
- queries: bfloat16 [8, 2, 2048, 4096], P('section', None, 'seq'), may hold values from -6 to 6
- gain: float32 [8, 4096], P('section'), may hold values from 0.5 to 2
- key_weight: bfloat16 [8, 4096, 512], P('section'), may hold values from -1 to 1
- value_weight: bfloat16 [8, 4096, 512], P('section'), may hold values from -0.09375 to 0.09375
- tree_ids: int32 [2, 2048], replicated, may hold values from 0 to 7, as said below
- branch_ids: int32 [2, 2048], replicated, may hold values from 0 to 2, as said below
- span_order: int32 [2, 32], replicated, may hold values from 0 to 31, each once within a row
Outputs:
- layer_out: bfloat16 [8, 2, 2048, 4096], P('section', None, 'seq')
Inputs may be any that keep to these rules, and one draw needn't show every extreme that they name: `tree_ids`: in each microbatch nondecreasing along the packed positions, every value of 0 to 7 present, each tree a multiple of 16 positions long. `branch_ids`: within each tree the prompt, chosen and rejected positions come in that order, each branch one position or more. `span_order`: each row is a permutation of 0 to 31.
All inputs are finite; a program needn't handle non-finite values.
Results may differ from a plain program's by a relative error of at most 0.02.
Values may be sent and summed in bfloat16 or wider, within the bound.
No kernel may reach another device: no remote copies, remote signals or barrier semaphores. Data moves between devices by JAX's collectives and lax.ppermute only.
A program may use at most 128 MiB of HBM per device.

v0:
```python
import math
import jax
import jax.numpy as jnp
from jax import lax
from jax.sharding import PartitionSpec as P

HQ = 32
HK = 4
HD = 128
SPAN = 64
rope_base = 500000.0


def from_behind(value, axis, by):
    size = lax.axis_size(axis)
    pairs = [(i, i + by) for i in range(size) if 0 <= i + by < size]
    return lax.ppermute(value, axis, pairs)


def frequencies():
    exponent = jnp.arange(HD // 2, dtype=jnp.float32) * (2.0 / HD)
    return jnp.power(jnp.float32(rope_base), -exponent)


def rotate(vectors, angles):
    half_dim = vectors.shape[-1] // 2
    cosine = jnp.cos(angles)[..., None, :]
    sine_part = jnp.sin(angles)[..., None, :]
    lower_half = vectors[..., :half_dim]
    upper_half = vectors[..., half_dim:]
    return jnp.concatenate(
        [
            lower_half * cosine - upper_half * sine_part,
            upper_half * cosine + lower_half * sine_part,
        ],
        axis=-1,
    )


def tree_positions(tree_ids, branch_ids):
    positions = jnp.arange(tree_ids.shape[1], dtype=jnp.int32)[None, :]
    opening = jnp.concatenate(
        [jnp.ones_like(tree_ids[:, :1]), (tree_ids[:, 1:] != tree_ids[:, :-1]).astype(jnp.int32)],
        axis=1,
    )
    starts = lax.cummax(jnp.where(opening > 0, positions, 0), axis=1)
    chosen = (branch_ids == 1).astype(jnp.int32)
    counted = jnp.cumsum(chosen, axis=1, dtype=jnp.int32)
    before = jnp.take_along_axis(counted - chosen, starts, axis=1)
    skipped = jnp.where(branch_ids == 2, counted - before, 0)
    return positions - starts - skipped


def local(hidden, queries, gain, key_weight, value_weight, tree_ids, branch_ids, span_order):
    section_id = lax.axis_index("section")
    shard_id = lax.axis_index("seq")
    section_count = lax.axis_size("section")
    micro_count, row_count, model_width = hidden.shape
    seq_len = tree_ids.shape[1]
    per_pass = 1
    ratio = HQ // HK
    scale = 1.0 / math.sqrt(HD)
    rotary_all = tree_positions(tree_ids, branch_ids)
    stored_ids = jnp.arange(seq_len, dtype=jnp.int32)
    packed_all = jnp.take(span_order, stored_ids // SPAN, axis=1) * SPAN + stored_ids % SPAN
    inverse = frequencies()
    gain_row = gain[0]
    key_mat = key_weight[0]
    value_mat = value_weight[0]

    def run_layer(current, first_mb, active):
        packed = lax.dynamic_slice_in_dim(packed_all, first_mb, per_pass, 0)
        trees = lax.dynamic_slice_in_dim(tree_ids, first_mb, per_pass, 0)
        branches = lax.dynamic_slice_in_dim(branch_ids, first_mb, per_pass, 0)
        rotary = lax.dynamic_slice_in_dim(rotary_all, first_mb, per_pass, 0)
        own_packed = lax.dynamic_slice_in_dim(packed, shard_id * row_count, row_count, 1)
        own_tree = jnp.take_along_axis(trees, own_packed, axis=1)
        own_branch = jnp.take_along_axis(branches, own_packed, axis=1)
        own_angles = (
            jnp.take_along_axis(rotary, own_packed, axis=1).astype(jnp.float32)[..., None] * inverse
        )
        widened = current.astype(jnp.float32)
        norm_scale = lax.rsqrt(jnp.mean(widened * widened, axis=-1, keepdims=True) + 1e-05)
        normed = (widened * norm_scale * gain_row).astype(jnp.bfloat16)
        flat = normed.reshape(per_pass * row_count, model_width)
        key_proj = jnp.dot(flat, key_mat, preferred_element_type=jnp.float32).reshape(
            per_pass, row_count, HK, HD
        )
        key_rows = (
            rotate(key_proj, own_angles).astype(jnp.bfloat16).reshape(per_pass, row_count, HK * HD)
        )
        value_rows = (
            jnp.dot(flat, value_mat, preferred_element_type=jnp.float32)
            .astype(jnp.bfloat16)
            .reshape(per_pass, row_count, HK * HD)
        )
        query_local = lax.dynamic_slice_in_dim(queries[0], first_mb, per_pass, 0)
        turned = rotate(
            query_local.astype(jnp.float32).reshape(per_pass, row_count, HQ, HD), own_angles
        ).astype(jnp.bfloat16)
        grouped = turned.reshape(per_pass, row_count, HK, ratio, HD)
        start_top = jnp.full((per_pass, HK, ratio, row_count), -jnp.inf, jnp.float32)
        start_sum = jnp.zeros((per_pass, HK, ratio, row_count), jnp.float32)
        start_acc = jnp.zeros((per_pass, HK, ratio, row_count, HD), jnp.float32)
        key_piece = lax.all_gather(key_rows, "seq", axis=1, tiled=True)
        value_piece = lax.all_gather(value_rows, "seq", axis=1, tiled=True)
        piece_len = key_piece.shape[1]
        block_len = math.gcd(piece_len, 512)

        def update(inner, operands):
            row_top, denominator, accum = inner
            key_blk, value_blk, allowed = operands
            scores = (
                jnp.einsum(
                    "grkhd,gskd->gkhrs",
                    grouped,
                    key_blk.reshape(per_pass, block_len, HK, HD),
                    preferred_element_type=jnp.float32,
                )
                * scale
            )
            masked = jnp.where(allowed[:, None, None], scores, -jnp.inf)
            new_top = jnp.maximum(row_top, jnp.max(masked, axis=-1))
            safe_top = jnp.where(jnp.isfinite(new_top), new_top, 0.0)
            weights = jnp.exp(masked - safe_top[..., None])
            rescale = jnp.exp(row_top - safe_top)
            denominator = denominator * rescale + jnp.sum(weights, axis=-1)
            accum = accum * rescale[..., None] + jnp.einsum(
                "gkhrs,gskd->gkhrd",
                weights.astype(jnp.bfloat16),
                value_blk.reshape(per_pass, block_len, HK, HD),
                preferred_element_type=jnp.float32,
            )
            return (new_top, denominator, accum)

        def step(block_id, inner):
            begin = block_id * block_len
            key_blk = lax.dynamic_slice_in_dim(key_piece, begin, block_len, 1)
            value_blk = lax.dynamic_slice_in_dim(value_piece, begin, block_len, 1)
            key_packed = lax.dynamic_slice_in_dim(packed, begin, block_len, 1)
            key_tree = jnp.take_along_axis(trees, key_packed, axis=1)
            key_branch = jnp.take_along_axis(branches, key_packed, axis=1)
            allowed = (
                (own_tree[:, :, None] == key_tree[:, None, :])
                & (key_packed[:, None, :] <= own_packed[:, :, None])
                & (
                    (key_branch[:, None, :] == 0)
                    | (key_branch[:, None, :] == own_branch[:, :, None])
                )
            )
            operands = (key_blk, value_blk, allowed)
            return update(inner, operands)

        def sweep(inner):
            return lax.fori_loop(0, piece_len // block_len, step, inner)

        row_top, denominator, accum = lax.cond(
            active, sweep, lambda inner: inner, (start_top, start_sum, start_acc)
        )
        safe_sum = jnp.where(denominator > 0.0, denominator, 1.0)
        attended = (
            (accum / safe_sum[..., None])
            .transpose(0, 3, 1, 2, 4)
            .reshape(per_pass, row_count, HQ * HD)
            .astype(jnp.bfloat16)
        )
        return (widened + attended.astype(jnp.float32)).astype(jnp.bfloat16)

    tick_count = section_count + micro_count // per_pass - 1

    def advance(step_id, state_pair):
        previous, outputs = state_pair
        incoming = from_behind(previous, "section", 1)
        first_mb = (step_id - section_id) * per_pass
        active = (first_mb >= 0) & (first_mb < micro_count)
        start_at = jnp.clip(first_mb, 0, micro_count - per_pass)
        entering = lax.dynamic_slice_in_dim(hidden, start_at, per_pass, 0)
        current = jnp.where(section_id == 0, entering, incoming)
        computed = run_layer(current, start_at, active)
        result = jnp.where(active, computed, jnp.zeros_like(computed))
        stored = lax.dynamic_update_slice_in_dim(outputs, result, start_at, 0)
        outputs = jnp.where(active, stored, outputs)
        return (result, outputs)

    empty_pass = jnp.zeros((per_pass, row_count, model_width), jnp.bfloat16)
    empty_out = jnp.zeros((micro_count, row_count, model_width), jnp.bfloat16)
    final_pass, outputs = lax.fori_loop(0, tick_count, advance, (empty_pass, empty_out))
    return outputs[None]


def solution(mesh):
    placed = (
        P(None, "seq", None),
        P("section", None, "seq", None),
        P("section", None),
        P("section", None, None),
        P("section", None, None),
        P(),
        P(),
        P(),
    )
    return jax.shard_map(
        local,
        mesh=mesh,
        in_specs=placed,
        out_specs=P("section", None, "seq", None),
        check_vma=False,
    )
```

profile of v0, /device:TPU:25, one launch (start us, length us, event | category | flops | bytes accessed | tf_op | source)
XLA Modules:
  0.0 2184.3 jit_solution(5759646535908856767)
XLA Ops:
  6.5 6.4 copy.28
  15.4 34.9 %gather_fusion.6 = s32[4096]{0:T(1024)S(1)} fusion(s32[2,2048]{1,0:T(2,128)S(1)} %bitcast_subtract_fusion, s32[4096]{0:T(1024)S(1)} %bitcast.243), kind=kCustom, calls=%fused_computation.6 | custom fusion | bytes 65536 | tf_op jit(solution)/shard_map/jit(take_along_axis)/gather | solution.py:49
  50.5 5.5 gather_fusion.5
  58.6 2118.9 %while.41 = (s32[]{:T(128)}, bf16[1,128,4096]{2,1,0:T(8,128)(2,1)}, bf16[2,128,4096]{2,1,0:T(8,128)(2,1)}, s32[]{:T(128)}, pred[]{:T(512)}, /*index=5*/bf16[2,12...) while((s32[]{:T(128)}, bf16[1,128,4096]{2,1,0:T(8,128)(2,1)}, ...), condition=%wide.region_12.15_spmd.clone, body=%wide.region_4.14_spmd.clone.sunk | while | flops 2188912640 | bytes 114081576 | solution.py:187
  80.2 49.8 %all-gather.7.cloned.1.call-done = bf16[1,2048,512]{1,2,0:T(8,128)(2,1)} async-done(((bf16[1,128,512]{1,2,0:T(8,128)(2,1)}), bf16[1,2048,512]{1,2,0:T(8,128)(2,1)}) %all-gather.7.cloned.1.call-update) | async-done | bytes 2097168 | tf_op jit(solution)/shard_map/while/body/eval_jaxpr/all_gather | solution.py:105
  130.0 46.5 %all-gather.9.cloned.1.call-done = bf16[2048,512]{1,0:T(8,128)(2,1)} async-done(((bf16[128,512]{1,0:T(8,128)(2,1)}), bf16[2048,512]{1,0:T(8,128)(2,1)}) %all-gather.9.cloned.1.call-update) | async-done | bytes 2097168 | tf_op jit(solution)/shard_map/while/body/eval_jaxpr/all_gather | solution.py:106
  212.5 140.5 %all-gather.7.cloned.1.call-done = bf16[1,2048,512]{1,2,0:T(8,128)(2,1)} async-done(((bf16[1,128,512]{1,2,0:T(8,128)(2,1)}), bf16[1,2048,512]{1,2,0:T(8,128)(2,1)}) %all-gather.7.cloned.1.call-update) | async-done | bytes 2097168 | tf_op jit(solution)/shard_map/while/body/eval_jaxpr/all_gather | solution.py:105
  353.0 46.4 %all-gather.9.cloned.1.call-done = bf16[2048,512]{1,0:T(8,128)(2,1)} async-done(((bf16[128,512]{1,0:T(8,128)(2,1)}), bf16[2048,512]{1,0:T(8,128)(2,1)}) %all-gather.9.cloned.1.call-update) | async-done | bytes 2097168 | tf_op jit(solution)/shard_map/while/body/eval_jaxpr/all_gather | solution.py:106
  435.4 151.1 %all-gather.7.cloned.1.call-done = bf16[1,2048,512]{1,2,0:T(8,128)(2,1)} async-done(((bf16[1,128,512]{1,2,0:T(8,128)(2,1)}), bf16[1,2048,512]{1,2,0:T(8,128)(2,1)}) %all-gather.7.cloned.1.call-update) | async-done | bytes 2097168 | tf_op jit(solution)/shard_map/while/body/eval_jaxpr/all_gather | solution.py:105
  586.6 46.4 %all-gather.9.cloned.1.call-done = bf16[2048,512]{1,0:T(8,128)(2,1)} async-done(((bf16[128,512]{1,0:T(8,128)(2,1)}), bf16[2048,512]{1,0:T(8,128)(2,1)}) %all-gather.9.cloned.1.call-update) | async-done | bytes 2097168 | tf_op jit(solution)/shard_map/while/body/eval_jaxpr/all_gather | solution.py:106
  669.0 154.0 %all-gather.7.cloned.1.call-done = bf16[1,2048,512]{1,2,0:T(8,128)(2,1)} async-done(((bf16[1,128,512]{1,2,0:T(8,128)(2,1)}), bf16[1,2048,512]{1,2,0:T(8,128)(2,1)}) %all-gather.7.cloned.1.call-update) | async-done | bytes 2097168 | tf_op jit(solution)/shard_map/while/body/eval_jaxpr/all_gather | solution.py:105
  822.9 46.5 %all-gather.9.cloned.1.call-done = bf16[2048,512]{1,0:T(8,128)(2,1)} async-done(((bf16[128,512]{1,0:T(8,128)(2,1)}), bf16[2048,512]{1,0:T(8,128)(2,1)}) %all-gather.9.cloned.1.call-update) | async-done | bytes 2097168 | tf_op jit(solution)/shard_map/while/body/eval_jaxpr/all_gather | solution.py:106
  905.4 154.0 %all-gather.7.cloned.1.call-done = bf16[1,2048,512]{1,2,0:T(8,128)(2,1)} async-done(((bf16[1,128,512]{1,2,0:T(8,128)(2,1)}), bf16[1,2048,512]{1,2,0:T(8,128)(2,1)}) %all-gather.7.cloned.1.call-update) | async-done | bytes 2097168 | tf_op jit(solution)/shard_map/while/body/eval_jaxpr/all_gather | solution.py:105
  1059.4 46.4 %all-gather.9.cloned.1.call-done = bf16[2048,512]{1,0:T(8,128)(2,1)} async-done(((bf16[128,512]{1,0:T(8,128)(2,1)}), bf16[2048,512]{1,0:T(8,128)(2,1)}) %all-gather.9.cloned.1.call-update) | async-done | bytes 2097168 | tf_op jit(solution)/shard_map/while/body/eval_jaxpr/all_gather | solution.py:106
  1141.8 155.5 %all-gather.7.cloned.1.call-done = bf16[1,2048,512]{1,2,0:T(8,128)(2,1)} async-done(((bf16[1,128,512]{1,2,0:T(8,128)(2,1)}), bf16[1,2048,512]{1,2,0:T(8,128)(2,1)}) %all-gather.7.cloned.1.call-update) | async-done | bytes 2097168 | tf_op jit(solution)/shard_map/while/body/eval_jaxpr/all_gather | solution.py:105
  1297.3 46.4 %all-gather.9.cloned.1.call-done = bf16[2048,512]{1,0:T(8,128)(2,1)} async-done(((bf16[128,512]{1,0:T(8,128)(2,1)}), bf16[2048,512]{1,0:T(8,128)(2,1)}) %all-gather.9.cloned.1.call-update) | async-done | bytes 2097168 | tf_op jit(solution)/shard_map/while/body/eval_jaxpr/all_gather | solution.py:106
  1379.7 155.5 %all-gather.7.cloned.1.call-done = bf16[1,2048,512]{1,2,0:T(8,128)(2,1)} async-done(((bf16[1,128,512]{1,2,0:T(8,128)(2,1)}), bf16[1,2048,512]{1,2,0:T(8,128)(2,1)}) %all-gather.7.cloned.1.call-update) | async-done | bytes 2097168 | tf_op jit(solution)/shard_map/while/body/eval_jaxpr/all_gather | solution.py:105
  1535.2 46.4 %all-gather.9.cloned.1.call-done = bf16[2048,512]{1,0:T(8,128)(2,1)} async-done(((bf16[128,512]{1,0:T(8,128)(2,1)}), bf16[2048,512]{1,0:T(8,128)(2,1)}) %all-gather.9.cloned.1.call-update) | async-done | bytes 2097168 | tf_op jit(solution)/shard_map/while/body/eval_jaxpr/all_gather | solution.py:106
  1597.8 111.5 %collective-permute-done = bf16[1,128,4096]{2,1,0:T(8,128)(2,1)S(1)} collective-permute-done((bf16[1,128,4096]{2,1,0:T(8,128)(2,1)S(1)}, bf16[1,128,4096]{2,1,0:T(8,128)(2,1)S(1)}, u32[]{:S(2)}, u32[]{:S(2)}) %collective-permute-start) | collective-permute-done | bytes 1048608 | tf_op jit(solution)/shard_map/while/body/eval_jaxpr/ppermute | solution.py:17
  1726.1 46.7 %all-gather.7.cloned.1.call-done = bf16[1,2048,512]{1,2,0:T(8,128)(2,1)} async-done(((bf16[1,128,512]{1,2,0:T(8,128)(2,1)}), bf16[1,2048,512]{1,2,0:T(8,128)(2,1)}) %all-gather.7.cloned.1.call-update) | async-done | bytes 2097168 | tf_op jit(solution)/shard_map/while/body/eval_jaxpr/all_gather | solution.py:105
  1772.8 46.4 %all-gather.9.cloned.1.call-done = bf16[2048,512]{1,0:T(8,128)(2,1)} async-done(((bf16[128,512]{1,0:T(8,128)(2,1)}), bf16[2048,512]{1,0:T(8,128)(2,1)}) %all-gather.9.cloned.1.call-update) | async-done | bytes 2097168 | tf_op jit(solution)/shard_map/while/body/eval_jaxpr/all_gather | solution.py:106
  1819.1 110.7 %conditional.3 = (f32[1,4,8,128]{3,2,1,0:T(8,128)}, f32[1,4,8,128,128]{4,3,2,1,0:T(8,128)}) conditional(s32[]{:T(128)} %convert_element_type.273, () %tuple.129, (s32[2,2048]{1,0:T(2,128)S(1)}, s32[]{:T(128)}, pred[1,128]{1,0:T(4,128)(4,1)S(1)}, s32[1,2048]{1,0:T(1,128)S(1)}, s32[1,128]{1,0:T(1,128)S(1)}, /*index=5*/s32[1,2048]{1,0:T(1,128)S(1)}, ...), branch_computations={%region_6.7_spmd, %region_7.13_spmd.clone} | conditional | flops 1098833152 | bytes 35224720 | solution.py:157
  1819.2 110.7 %while.40 = (s32[]{:T(128)}, f32[1,4,8,128]{3,2,1,0:T(8,128)S(1)}, f32[1,4,8,128]{3,2,1,0:T(8,128)}, f32[1,4,8,128,128]{4,3,2,1,0:T(8,128)}, s32[1,128]{1,0:T(1,...) while((s32[]{:T(128)}, f32[1,4,8,128]{3,2,1,0:T(8,128)S(1)}, ...), condition=%wide.region_11.12_spmd.clone, body=%wide.region_8.11_spmd.clone.sunk | while | flops 1098832896 | bytes 35205864 | solution.py:155
  1827.0 4.6 fusion.86
  1831.6 5.1 fusion.89
  1838.6 7.3 bitcast_add_fusion.5
  1853.6 4.6 fusion.86
  1858.3 5.1 fusion.89
  1866.0 7.9 bitcast_add_fusion.5
  1881.6 4.6 fusion.86
  1886.3 5.1 fusion.89
  1894.0 7.9 bitcast_add_fusion.5
  1909.6 4.6 fusion.86
  1914.3 5.1 fusion.89
  1922.0 7.9 bitcast_add_fusion.5
  1963.7 46.7 %all-gather.7.cloned.1.call-done = bf16[1,2048,512]{1,2,0:T(8,128)(2,1)} async-done(((bf16[1,128,512]{1,2,0:T(8,128)(2,1)}), bf16[1,2048,512]{1,2,0:T(8,128)(2,1)}) %all-gather.7.cloned.1.call-update) | async-done | bytes 2097168 | tf_op jit(solution)/shard_map/while/body/eval_jaxpr/all_gather | solution.py:105
  2010.4 46.4 %all-gather.9.cloned.1.call-done = bf16[2048,512]{1,0:T(8,128)(2,1)} async-done(((bf16[128,512]{1,0:T(8,128)(2,1)}), bf16[2048,512]{1,0:T(8,128)(2,1)}) %all-gather.9.cloned.1.call-update) | async-done | bytes 2097168 | tf_op jit(solution)/shard_map/while/body/eval_jaxpr/all_gather | solution.py:106
  2056.7 110.7 %conditional.3 = (f32[1,4,8,128]{3,2,1,0:T(8,128)}, f32[1,4,8,128,128]{4,3,2,1,0:T(8,128)}) conditional(s32[]{:T(128)} %convert_element_type.273, () %tuple.129, (s32[2,2048]{1,0:T(2,128)S(1)}, s32[]{:T(128)}, pred[1,128]{1,0:T(4,128)(4,1)S(1)}, s32[1,2048]{1,0:T(1,128)S(1)}, s32[1,128]{1,0:T(1,128)S(1)}, /*index=5*/s32[1,2048]{1,0:T(1,128)S(1)}, ...), branch_computations={%region_6.7_spmd, %region_7.13_spmd.clone} | conditional | flops 1098833152 | bytes 35224720 | solution.py:157
  2056.8 110.7 %while.40 = (s32[]{:T(128)}, f32[1,4,8,128]{3,2,1,0:T(8,128)S(1)}, f32[1,4,8,128]{3,2,1,0:T(8,128)}, f32[1,4,8,128,128]{4,3,2,1,0:T(8,128)}, s32[1,128]{1,0:T(1,...) while((s32[]{:T(128)}, f32[1,4,8,128]{3,2,1,0:T(8,128)S(1)}, ...), condition=%wide.region_11.12_spmd.clone, body=%wide.region_8.11_spmd.clone.sunk | while | flops 1098832896 | bytes 35205864 | solution.py:155
  2064.6 4.6 fusion.86
  2069.2 5.1 fusion.89
  2076.2 7.3 bitcast_add_fusion.5
  2095.9 5.1 fusion.89
  2103.6 7.9 bitcast_add_fusion.5
  2123.9 5.1 fusion.89
  2131.6 7.9 bitcast_add_fusion.5
  2151.9 5.1 fusion.89
  2159.6 7.9 bitcast_add_fusion.5
  (515 shorter events, 428.6 us)
Async XLA Ops:
  6.5 6.4 copy-start.1
  6.5 7.5 copy-start.2
  15.4 35.0 %copy-start.3 = (s32[2,32]{1,0:T(2,128)S(1)}, s32[2,32]{1,0:T(2,128)}, u32[]{:S(2)}) copy-start(s32[2,32]{1,0:T(2,128)} %param.25) | copy-start | bytes 772
  56.7 1.9 copy-start.4
  58.6 71.3 %all-gather.7.cloned.1.call-start = ((), (), s32[]{:S(2)}) async-start(), calls=%async_computation | async-start | bytes 2228224 | tf_op jit(solution)/shard_map/while/body/eval_jaxpr/all_gather | solution.py:105
  58.7 4.7 collective-permute-start
  69.4 107.1 %all-gather.9.cloned.1.call-start = ((), (), s32[]{:S(2)}) async-start(), calls=%async_computation.1 | async-start | bytes 2228224 | tf_op jit(solution)/shard_map/while/body/eval_jaxpr/all_gather | solution.py:106
  69.4 4.0 copy-start
  188.7 164.3 %all-gather.7.cloned.1.call-start = ((), (), s32[]{:S(2)}) async-start(), calls=%async_computation | async-start | bytes 2228224 | tf_op jit(solution)/shard_map/while/body/eval_jaxpr/all_gather | solution.py:105
  190.0 5.8 collective-permute-start
  201.7 197.6 %all-gather.9.cloned.1.call-start = ((), (), s32[]{:S(2)}) async-start(), calls=%async_computation.1 | async-start | bytes 2228224 | tf_op jit(solution)/shard_map/while/body/eval_jaxpr/all_gather | solution.py:106
  201.8 4.0 copy-start
  411.6 174.9 %all-gather.7.cloned.1.call-start = ((), (), s32[]{:S(2)}) async-start(), calls=%async_computation | async-start | bytes 2228224 | tf_op jit(solution)/shard_map/while/body/eval_jaxpr/all_gather | solution.py:105
  412.9 5.8 collective-permute-start
  424.6 208.3 %all-gather.9.cloned.1.call-start = ((), (), s32[]{:S(2)}) async-start(), calls=%async_computation.1 | async-start | bytes 2228224 | tf_op jit(solution)/shard_map/while/body/eval_jaxpr/all_gather | solution.py:106
  424.7 4.0 copy-start
  645.1 177.8 %all-gather.7.cloned.1.call-start = ((), (), s32[]{:S(2)}) async-start(), calls=%async_computation | async-start | bytes 2228224 | tf_op jit(solution)/shard_map/while/body/eval_jaxpr/all_gather | solution.py:105
  646.4 5.8 collective-permute-start
  658.2 211.2 %all-gather.9.cloned.1.call-start = ((), (), s32[]{:S(2)}) async-start(), calls=%async_computation.1 | async-start | bytes 2228224 | tf_op jit(solution)/shard_map/while/body/eval_jaxpr/all_gather | solution.py:106
  658.2 4.0 copy-start
  881.6 177.8 %all-gather.7.cloned.1.call-start = ((), (), s32[]{:S(2)}) async-start(), calls=%async_computation | async-start | bytes 2228224 | tf_op jit(solution)/shard_map/while/body/eval_jaxpr/all_gather | solution.py:105
  882.9 5.8 collective-permute-start
  894.7 211.1 %all-gather.9.cloned.1.call-start = ((), (), s32[]{:S(2)}) async-start(), calls=%async_computation.1 | async-start | bytes 2228224 | tf_op jit(solution)/shard_map/while/body/eval_jaxpr/all_gather | solution.py:106
  894.7 4.0 copy-start
  1118.0 179.3 %all-gather.7.cloned.1.call-start = ((), (), s32[]{:S(2)}) async-start(), calls=%async_computation | async-start | bytes 2228224 | tf_op jit(solution)/shard_map/while/body/eval_jaxpr/all_gather | solution.py:105
  1119.3 5.8 collective-permute-start
  1131.0 212.6 %all-gather.9.cloned.1.call-start = ((), (), s32[]{:S(2)}) async-start(), calls=%async_computation.1 | async-start | bytes 2228224 | tf_op jit(solution)/shard_map/while/body/eval_jaxpr/all_gather | solution.py:106
  1131.1 4.0 copy-start
  1355.9 179.3 %all-gather.7.cloned.1.call-start = ((), (), s32[]{:S(2)}) async-start(), calls=%async_computation | async-start | bytes 2228224 | tf_op jit(solution)/shard_map/while/body/eval_jaxpr/all_gather | solution.py:105
  1357.2 5.8 collective-permute-start
  1368.9 212.6 %all-gather.9.cloned.1.call-start = ((), (), s32[]{:S(2)}) async-start(), calls=%async_computation.1 | async-start | bytes 2228224 | tf_op jit(solution)/shard_map/while/body/eval_jaxpr/all_gather | solution.py:106
  1369.0 4.0 copy-start
  1593.7 179.0 %all-gather.7.cloned.1.call-start = ((), (), s32[]{:S(2)}) async-start(), calls=%async_computation | async-start | bytes 2228224 | tf_op jit(solution)/shard_map/while/body/eval_jaxpr/all_gather | solution.py:105
  1595.0 114.3 %collective-permute-start = (bf16[1,128,4096]{2,1,0:T(8,128)(2,1)S(1)}, bf16[1,128,4096]{2,1,0:T(8,128)(2,1)S(1)}, u32[]{:S(2)}, u32[]{:S(2)}) collective-permute-start(bf16[1,128,4096]{2,1,0:T(8,128)(2,1)S(1)} %broadcast_select_fusion.7), channel_id=1, source_target_pairs={{0,16},{16,32},{32,48},{48,64},{64,80},{80,96},{96,112},{1,17},{17... | collective-permute-start | bytes 3145736 | tf_op jit(solution)/shard_map/while/body/eval_jaxpr/ppermute | solution.py:17
  1715.3 103.8 %all-gather.9.cloned.1.call-start = ((), (), s32[]{:S(2)}) async-start(), calls=%async_computation.1 | async-start | bytes 2228224 | tf_op jit(solution)/shard_map/while/body/eval_jaxpr/all_gather | solution.py:106
  1715.4 4.0 copy-start
  1939.9 70.5 %all-gather.7.cloned.1.call-start = ((), (), s32[]{:S(2)}) async-start(), calls=%async_computation | async-start | bytes 2228224 | tf_op jit(solution)/shard_map/while/body/eval_jaxpr/all_gather | solution.py:105
  1941.2 5.8 collective-permute-start
  1952.9 103.8 %all-gather.9.cloned.1.call-start = ((), (), s32[]{:S(2)}) async-start(), calls=%async_computation.1 | async-start | bytes 2228224 | tf_op jit(solution)/shard_map/while/body/eval_jaxpr/all_gather | solution.py:106
  1953.0 4.0 copy-start
Sparse Core Ops, SparseCore 0:
  69.5 60.4 all-gather.6
  132.1 44.3 all-gather.8
  201.9 151.1 all-gather.6
  355.0 44.3 all-gather.8
  424.8 161.7 all-gather.6
  588.5 44.3 all-gather.8
  658.3 164.5 all-gather.6
  825.0 44.3 all-gather.8
  894.8 164.5 all-gather.6
  1061.4 44.3 all-gather.8
  1131.1 166.0 all-gather.6
  1299.3 44.3 all-gather.8
  1369.0 166.0 all-gather.6
  1537.1 44.3 all-gather.8
  1715.4 57.2 all-gather.6
  1774.8 44.3 all-gather.8
  1953.0 57.2 all-gather.6
  2012.4 44.3 all-gather.8
where the time goes:
time: 2190 us; the launch traced here: 2180 us
  waiting for transfers between devices  1610 us (74%)
  local copies, waits for them, and re-layouts  215 us (10%)
  other arithmetic  171 us (8%)
  matrix products  164 us (7%)
    all_gather x9, waiting for transfers between devices, run_layer(): key_piece = lax.all_gather(key_rows, 'seq', axis=1, tiled=True)  1050 us
    all_gather x9, waiting for transfers between devices, run_layer(): value_piece = lax.all_gather(value_rows, 'seq', axis=1, tiled=True)  418 us
    ppermute x9, waiting for transfers between devices, from_behind(): return lax.ppermute(value, axis, pairs)  134 us
    dot_general x8, matrix products, update(): jnp.einsum('gkhrs,gskd->gkhrd', weights.astype(jnp.bfloat16), value_blk.r...  61.6 us
  transfers between devices with their start and end apart: 27, of which 27 were waited for; matrix products, arithmetic and copies ran while one was open for 5% of the time, Pallas kernels for 0%

commit v1 on v0

--- a/solution.py
+++ b/solution.py
@@ -102,7 +102,9 @@
         start_top = jnp.full((per_pass, HK, ratio, row_count), -jnp.inf, jnp.float32)
         start_sum = jnp.zeros((per_pass, HK, ratio, row_count), jnp.float32)
         start_acc = jnp.zeros((per_pass, HK, ratio, row_count, HD), jnp.float32)
-        key_piece = lax.all_gather(key_rows, "seq", axis=1, tiled=True)
+        key_piece = jnp.concatenate(
+            lax.all_to_all(jnp.stack([key_rows] * lax.axis_size("seq")), "seq", 0, 0), axis=1
+        )
         value_piece = lax.all_gather(value_rows, "seq", axis=1, tiled=True)
         piece_len = key_piece.shape[1]
         block_len = math.gcd(piece_len, 512)

time: 2190 us -> 1880 us (0.86)
  waiting for transfers between devices: 1610 us -> 1230 us
  starting transfers between devices: 12 us -> 58.2 us
  local copies, waits for them, and re-layouts: 215 us -> 237 us
    all_gather x9 -> x0, waiting for transfers between devices: 1050 us -> none  [run_layer(): key_piece = lax.all_gather(key_rows, 'seq', axis=1, tiled=True)]
    all_gather x9, waiting for transfers between devices: 418 us -> 954 us  [run_layer(): value_piece = lax.all_gather(value_rows, 'seq', axis=1, tiled=True)]
    all_to_all x0 -> x9, waiting for transfers between devices: none -> 129 us  [run_layer(): lax.all_to_all(jnp.stack([key_rows] * lax.axis_size('seq')), 'seq', 0, 0)]
    all_to_all x0 -> x9, starting transfers between devices: none -> 46.5 us  [run_layer(): lax.all_to_all(jnp.stack([key_rows] * lax.axis_size('seq')), 'seq', 0, 0)]
  transfers between devices with their start and end apart: 27 -> 27, of which waited for: 27 -> 27; matrix products, arithmetic and copies ran while one was open for 5% -> 7% of each run, Pallas kernels for 0% -> 0%
where the time goes in v1:
time: 1880 us; the launch traced here: 1870 us
  waiting for transfers between devices  1230 us (65%)
  local copies, waits for them, and re-layouts  237 us (13%)
  other arithmetic  165 us (9%)
  matrix products  163 us (9%)
  starting transfers between devices  58.2 us (3%)
    all_gather x9, waiting for transfers between devices, run_layer(): value_piece = lax.all_gather(value_rows, 'seq', axis=1, tiled=True)  954 us
    ppermute x9, waiting for transfers between devices, from_behind(): return lax.ppermute(value, axis, pairs)  151 us
    all_to_all x9, waiting for transfers between devices, run_layer(): lax.all_to_all(jnp.stack([key_rows] * lax.axis_size('seq')), 'seq', 0, 0)  129 us
    dot_general x8, matrix products, update(): jnp.einsum('gkhrs,gskd->gkhrd', weights.astype(jnp.bfloat16), value_blk.r...  61.4 us
    all_to_all x9, starting transfers between devices, run_layer(): lax.all_to_all(jnp.stack([key_rows] * lax.axis_size('seq')), 'seq', 0, 0)  46.5 us
    reduce_sum x8, other arithmetic, update(): denominator = denominator * rescale + jnp.sum(weights, axis=-1)  40.5 us
    convert_element_type x18, local copies, waits for them, and re-layouts, run_layer(): return (widened + attended.astype(jnp.float32)).astype(jnp.bfloat16)  38.7 us
  transfers between devices with their start and end apart: 27, of which 27 were waited for; matrix products, arithmetic and copies ran while one was open for 7% of the time, Pallas kernels for 0%

profile of v1, /device:TPU:25, one launch (start us, length us, event | category | flops | bytes accessed | tf_op | source)
XLA Modules:
  0.0 1874.1 jit_solution(15160680657312818172)
XLA Ops:
  6.5 6.4 copy.41
  15.4 34.9 %gather_fusion.6 = s32[4096]{0:T(1024)S(1)} fusion(s32[2,2048]{1,0:T(2,128)S(1)} %bitcast_subtract_fusion, s32[4096]{0:T(1024)S(1)} %bitcast.248), kind=kCustom, calls=%fused_computation.6 | custom fusion | bytes 65536 | tf_op jit(solution)/shard_map/jit(take_along_axis)/gather | solution.py:49
  50.5 5.5 gather_fusion.5
  58.6 1809.0 %while.41 = (s32[]{:T(128)}, bf16[1,128,4096]{2,1,0:T(8,128)(2,1)}, bf16[2,128,4096]{2,1,0:T(8,128)(2,1)}, s32[]{:T(128)}, pred[]{:T(512)}, /*index=5*/bf16[2,12...) while((s32[]{:T(128)}, bf16[1,128,4096]{2,1,0:T(8,128)(2,1)}, ...), condition=%wide.region_12.15_spmd.clone, body=%wide.region_4.14_spmd.clone.sunk | while | flops 2188912640 | bytes 120110880 | solution.py:189
  75.6 7.8 all-to-all-start
  90.4 15.0 all-to-all-done
  105.3 36.5 %all-gather.6.cloned.1.call-done = bf16[2048,512]{1,0:T(8,128)(2,1)} async-done(((bf16[128,512]{1,0:T(8,128)(2,1)}), bf16[2048,512]{1,0:T(8,128)(2,1)}) %all-gather.6.cloned.1.call-update) | async-done | bytes 2097168 | tf_op jit(solution)/shard_map/while/body/eval_jaxpr/all_gather | solution.py:108
  173.3 4.8 all-to-all-start
  185.1 14.3 all-to-all-done
  199.4 124.3 %all-gather.6.cloned.1.call-done = bf16[2048,512]{1,0:T(8,128)(2,1)} async-done(((bf16[128,512]{1,0:T(8,128)(2,1)}), bf16[2048,512]{1,0:T(8,128)(2,1)}) %all-gather.6.cloned.1.call-update) | async-done | bytes 2097168 | tf_op jit(solution)/shard_map/while/body/eval_jaxpr/all_gather | solution.py:108
  355.2 4.8 all-to-all-start
  366.9 14.3 all-to-all-done
  381.3 149.6 %all-gather.6.cloned.1.call-done = bf16[2048,512]{1,0:T(8,128)(2,1)} async-done(((bf16[128,512]{1,0:T(8,128)(2,1)}), bf16[2048,512]{1,0:T(8,128)(2,1)}) %all-gather.6.cloned.1.call-update) | async-done | bytes 2097168 | tf_op jit(solution)/shard_map/while/body/eval_jaxpr/all_gather | solution.py:108
  562.3 4.8 all-to-all-start
  574.1 14.3 all-to-all-done
  588.5 141.8 %all-gather.6.cloned.1.call-done = bf16[2048,512]{1,0:T(8,128)(2,1)} async-done(((bf16[128,512]{1,0:T(8,128)(2,1)}), bf16[2048,512]{1,0:T(8,128)(2,1)}) %all-gather.6.cloned.1.call-update) | async-done | bytes 2097168 | tf_op jit(solution)/shard_map/while/body/eval_jaxpr/all_gather | solution.py:108
  773.5 14.3 all-to-all-done
  787.8 144.5 %all-gather.6.cloned.1.call-done = bf16[2048,512]{1,0:T(8,128)(2,1)} async-done(((bf16[128,512]{1,0:T(8,128)(2,1)}), bf16[2048,512]{1,0:T(8,128)(2,1)}) %all-gather.6.cloned.1.call-update) | async-done | bytes 2097168 | tf_op jit(solution)/shard_map/while/body/eval_jaxpr/all_gather | solution.py:108
  975.7 14.3 all-to-all-done
  990.0 143.6 %all-gather.6.cloned.1.call-done = bf16[2048,512]{1,0:T(8,128)(2,1)} async-done(((bf16[128,512]{1,0:T(8,128)(2,1)}), bf16[2048,512]{1,0:T(8,128)(2,1)}) %all-gather.6.cloned.1.call-update) | async-done | bytes 2097168 | tf_op jit(solution)/shard_map/while/body/eval_jaxpr/all_gather | solution.py:108
  1176.9 13.0 all-to-all-done
  1189.8 150.9 %all-gather.6.cloned.1.call-done = bf16[2048,512]{1,0:T(8,128)(2,1)} async-done(((bf16[128,512]{1,0:T(8,128)(2,1)}), bf16[2048,512]{1,0:T(8,128)(2,1)}) %all-gather.6.cloned.1.call-update) | async-done | bytes 2097168 | tf_op jit(solution)/shard_map/while/body/eval_jaxpr/all_gather | solution.py:108
  1355.6 116.2 %collective-permute-done = bf16[1,128,4096]{2,1,0:T(8,128)(2,1)S(1)} collective-permute-done((bf16[1,128,4096]{2,1,0:T(8,128)(2,1)S(1)}, bf16[1,128,4096]{2,1,0:T(8,128)(2,1)S(1)}, u32[]{:S(2)}, u32[]{:S(2)}) %collective-permute-start) | collective-permute-done | bytes 1048608 | tf_op jit(solution)/shard_map/while/body/eval_jaxpr/ppermute | solution.py:17
  1483.9 4.8 all-to-all-start
  1495.7 15.0 all-to-all-done
  1510.7 32.2 %all-gather.6.cloned.1.call-done = bf16[2048,512]{1,0:T(8,128)(2,1)} async-done(((bf16[128,512]{1,0:T(8,128)(2,1)}), bf16[2048,512]{1,0:T(8,128)(2,1)}) %all-gather.6.cloned.1.call-update) | async-done | bytes 2097168 | tf_op jit(solution)/shard_map/while/body/eval_jaxpr/all_gather | solution.py:108
  1542.8 113.8 %conditional.3 = (f32[1,4,8,128]{3,2,1,0:T(8,128)}, f32[1,4,8,128,128]{4,3,2,1,0:T(8,128)}) conditional(s32[]{:T(128)} %convert_element_type.271, () %tuple.131, (bf16[16,1,128,512]{2,3,1,0:T(8,128)(2,1)}, s32[2,2048]{1,0:T(2,128)S(1)}, s32[]{:T(128)}, pred[1,128]{1,0:T(4,128)(4,1)S(1)}, s32[1,2048]{1,0:T(1,128)S(1)}, ...), branch_computations={%region_6.7_spmd, %region_7.13_spmd.clone} | conditional | flops 1098833152 | bytes 39419024 | solution.py:159
  1546.1 110.6 %while.40 = (s32[]{:T(128)}, f32[1,4,8,128]{3,2,1,0:T(8,128)S(1)}, f32[1,4,8,128]{3,2,1,0:T(8,128)}, f32[1,4,8,128,128]{4,3,2,1,0:T(8,128)}, s32[1,128]{1,0:T(1,...) while((s32[]{:T(128)}, f32[1,4,8,128]{3,2,1,0:T(8,128)S(1)}, ...), condition=%wide.region_11.12_spmd.clone, body=%wide.region_8.11_spmd.clone.sunk | while | flops 1098832896 | bytes 35205864 | solution.py:157
  1558.5 5.1 fusion.90
  1565.5 7.2 bitcast_add_fusion.5
  1585.2 5.1 fusion.90
  1592.9 7.8 bitcast_add_fusion.5
  1613.2 5.1 fusion.90
  1620.9 7.8 bitcast_add_fusion.5
  1641.1 5.1 fusion.90
  1648.8 7.8 bitcast_add_fusion.5
  1697.8 15.0 all-to-all-done
  1712.7 31.0 %all-gather.6.cloned.1.call-done = bf16[2048,512]{1,0:T(8,128)(2,1)} async-done(((bf16[128,512]{1,0:T(8,128)(2,1)}), bf16[2048,512]{1,0:T(8,128)(2,1)}) %all-gather.6.cloned.1.call-update) | async-done | bytes 2097168 | tf_op jit(solution)/shard_map/while/body/eval_jaxpr/all_gather | solution.py:108
  1743.7 113.8 %conditional.3 = (f32[1,4,8,128]{3,2,1,0:T(8,128)}, f32[1,4,8,128,128]{4,3,2,1,0:T(8,128)}) conditional(s32[]{:T(128)} %convert_element_type.271, () %tuple.131, (bf16[16,1,128,512]{2,3,1,0:T(8,128)(2,1)}, s32[2,2048]{1,0:T(2,128)S(1)}, s32[]{:T(128)}, pred[1,128]{1,0:T(4,128)(4,1)S(1)}, s32[1,2048]{1,0:T(1,128)S(1)}, ...), branch_computations={%region_6.7_spmd, %region_7.13_spmd.clone} | conditional | flops 1098833152 | bytes 39419024 | solution.py:159
  1747.0 110.6 %while.40 = (s32[]{:T(128)}, f32[1,4,8,128]{3,2,1,0:T(8,128)S(1)}, f32[1,4,8,128]{3,2,1,0:T(8,128)}, f32[1,4,8,128,128]{4,3,2,1,0:T(8,128)}, s32[1,128]{1,0:T(1,...) while((s32[]{:T(128)}, f32[1,4,8,128]{3,2,1,0:T(8,128)S(1)}, ...), condition=%wide.region_11.12_spmd.clone, body=%wide.region_8.11_spmd.clone.sunk | while | flops 1098832896 | bytes 35205864 | solution.py:157
  1759.4 5.1 fusion.90
  1766.4 7.2 bitcast_add_fusion.5
  1786.1 5.1 fusion.90
  1793.8 7.8 bitcast_add_fusion.5
  1814.1 5.1 fusion.90
  1821.8 7.8 bitcast_add_fusion.5
  1842.0 5.1 fusion.90
  1849.7 7.8 bitcast_add_fusion.5
  (517 shorter events, 497.6 us)
Async XLA Ops:
  6.5 6.4 copy-start.1
  6.5 7.5 copy-start.2
  15.4 35.0 %copy-start.3 = (s32[2,32]{1,0:T(2,128)S(1)}, s32[2,32]{1,0:T(2,128)}, u32[]{:S(2)}) copy-start(s32[2,32]{1,0:T(2,128)} %param.25) | copy-start | bytes 772
  56.7 1.9 copy-start.4
  58.6 83.2 %all-gather.6.cloned.1.call-start = ((), (), s32[]{:S(2)}) async-start(), calls=%async_computation.1 | async-start | bytes 2228224 | tf_op jit(solution)/shard_map/while/body/eval_jaxpr/all_gather | solution.py:108
  58.7 4.7 collective-permute-start
  75.6 8.0 copy-start
  75.6 29.7 %all-to-all-start = ((bf16[16,1,128,512]{2,3,1,0:T(8,128)(2,1)}), bf16[16,1,128,512]{2,3,1,0:T(8,128)(2,1)}, u32[]{:S(2)}, u32[]{:S(2)}) async-start(bf16[16,1,128,512]{2,3,1,0:T(8,128)(2,1)} %stack.7), calls=%async_computation | async-start | bytes 4194304 | tf_op jit(solution)/shard_map/while/body/eval_jaxpr/all_to_all | solution.py:106
  154.0 169.6 %all-gather.6.cloned.1.call-start = ((), (), s32[]{:S(2)}) async-start(), calls=%async_computation.1 | async-start | bytes 2228224 | tf_op jit(solution)/shard_map/while/body/eval_jaxpr/all_gather | solution.py:108
  155.3 5.8 collective-permute-start
  173.3 5.1 copy-start
  173.3 26.1 %all-to-all-start = ((bf16[16,1,128,512]{2,3,1,0:T(8,128)(2,1)}), bf16[16,1,128,512]{2,3,1,0:T(8,128)(2,1)}, u32[]{:S(2)}, u32[]{:S(2)}) async-start(bf16[16,1,128,512]{2,3,1,0:T(8,128)(2,1)} %stack.7), calls=%async_computation | async-start | bytes 4194304 | tf_op jit(solution)/shard_map/while/body/eval_jaxpr/all_to_all | solution.py:106
  335.9 195.0 %all-gather.6.cloned.1.call-start = ((), (), s32[]{:S(2)}) async-start(), calls=%async_computation.1 | async-start | bytes 2228224 | tf_op jit(solution)/shard_map/while/body/eval_jaxpr/all_gather | solution.py:108
  337.2 5.8 collective-permute-start
  355.2 5.1 copy-start
  355.2 26.1 %all-to-all-start = ((bf16[16,1,128,512]{2,3,1,0:T(8,128)(2,1)}), bf16[16,1,128,512]{2,3,1,0:T(8,128)(2,1)}, u32[]{:S(2)}, u32[]{:S(2)}) async-start(bf16[16,1,128,512]{2,3,1,0:T(8,128)(2,1)} %stack.7), calls=%async_computation | async-start | bytes 4194304 | tf_op jit(solution)/shard_map/while/body/eval_jaxpr/all_to_all | solution.py:106
  543.1 187.2 %all-gather.6.cloned.1.call-start = ((), (), s32[]{:S(2)}) async-start(), calls=%async_computation.1 | async-start | bytes 2228224 | tf_op jit(solution)/shard_map/while/body/eval_jaxpr/all_gather | solution.py:108
  544.4 5.8 collective-permute-start
  562.3 5.1 copy-start
  562.3 26.1 %all-to-all-start = ((bf16[16,1,128,512]{2,3,1,0:T(8,128)(2,1)}), bf16[16,1,128,512]{2,3,1,0:T(8,128)(2,1)}, u32[]{:S(2)}, u32[]{:S(2)}) async-start(bf16[16,1,128,512]{2,3,1,0:T(8,128)(2,1)} %stack.7), calls=%async_computation | async-start | bytes 4194304 | tf_op jit(solution)/shard_map/while/body/eval_jaxpr/all_to_all | solution.py:106
  742.5 189.9 %all-gather.6.cloned.1.call-start = ((), (), s32[]{:S(2)}) async-start(), calls=%async_computation.1 | async-start | bytes 2228224 | tf_op jit(solution)/shard_map/while/body/eval_jaxpr/all_gather | solution.py:108
  743.8 5.8 collective-permute-start
  761.7 5.1 copy-start
  761.8 26.1 %all-to-all-start = ((bf16[16,1,128,512]{2,3,1,0:T(8,128)(2,1)}), bf16[16,1,128,512]{2,3,1,0:T(8,128)(2,1)}, u32[]{:S(2)}, u32[]{:S(2)}) async-start(bf16[16,1,128,512]{2,3,1,0:T(8,128)(2,1)} %stack.7), calls=%async_computation | async-start | bytes 4194304 | tf_op jit(solution)/shard_map/while/body/eval_jaxpr/all_to_all | solution.py:106
  944.6 189.0 %all-gather.6.cloned.1.call-start = ((), (), s32[]{:S(2)}) async-start(), calls=%async_computation.1 | async-start | bytes 2228224 | tf_op jit(solution)/shard_map/while/body/eval_jaxpr/all_gather | solution.py:108
  945.9 5.8 collective-permute-start
  963.9 5.1 copy-start
  963.9 26.1 %all-to-all-start = ((bf16[16,1,128,512]{2,3,1,0:T(8,128)(2,1)}), bf16[16,1,128,512]{2,3,1,0:T(8,128)(2,1)}, u32[]{:S(2)}, u32[]{:S(2)}) async-start(bf16[16,1,128,512]{2,3,1,0:T(8,128)(2,1)} %stack.7), calls=%async_computation | async-start | bytes 4194304 | tf_op jit(solution)/shard_map/while/body/eval_jaxpr/all_to_all | solution.py:106
  1145.8 195.0 %all-gather.6.cloned.1.call-start = ((), (), s32[]{:S(2)}) async-start(), calls=%async_computation.1 | async-start | bytes 2228224 | tf_op jit(solution)/shard_map/while/body/eval_jaxpr/all_gather | solution.py:108
  1147.1 5.8 collective-permute-start
  1165.1 5.1 copy-start
  1165.1 24.7 %all-to-all-start = ((bf16[16,1,128,512]{2,3,1,0:T(8,128)(2,1)}), bf16[16,1,128,512]{2,3,1,0:T(8,128)(2,1)}, u32[]{:S(2)}, u32[]{:S(2)}) async-start(bf16[16,1,128,512]{2,3,1,0:T(8,128)(2,1)} %stack.7), calls=%async_computation | async-start | bytes 4194304 | tf_op jit(solution)/shard_map/while/body/eval_jaxpr/all_to_all | solution.py:106
  1353.0 189.9 %all-gather.6.cloned.1.call-start = ((), (), s32[]{:S(2)}) async-start(), calls=%async_computation.1 | async-start | bytes 2228224 | tf_op jit(solution)/shard_map/while/body/eval_jaxpr/all_gather | solution.py:108
  1354.3 117.5 %collective-permute-start = (bf16[1,128,4096]{2,1,0:T(8,128)(2,1)S(1)}, bf16[1,128,4096]{2,1,0:T(8,128)(2,1)S(1)}, u32[]{:S(2)}, u32[]{:S(2)}) collective-permute-start(bf16[1,128,4096]{2,1,0:T(8,128)(2,1)S(1)} %broadcast_select_fusion.7), channel_id=1, source_target_pairs={{0,16},{16,32},{32,48},{48,64},{64,80},{80,96},{96,112},{1,17},{17... | collective-permute-start | bytes 3145736 | tf_op jit(solution)/shard_map/while/body/eval_jaxpr/ppermute | solution.py:17
  1483.9 5.1 copy-start
  1483.9 26.7 %all-to-all-start = ((bf16[16,1,128,512]{2,3,1,0:T(8,128)(2,1)}), bf16[16,1,128,512]{2,3,1,0:T(8,128)(2,1)}, u32[]{:S(2)}, u32[]{:S(2)}) async-start(bf16[16,1,128,512]{2,3,1,0:T(8,128)(2,1)} %stack.7), calls=%async_computation | async-start | bytes 4194304 | tf_op jit(solution)/shard_map/while/body/eval_jaxpr/all_to_all | solution.py:106
  1666.7 77.0 %all-gather.6.cloned.1.call-start = ((), (), s32[]{:S(2)}) async-start(), calls=%async_computation.1 | async-start | bytes 2228224 | tf_op jit(solution)/shard_map/while/body/eval_jaxpr/all_gather | solution.py:108
  1668.0 5.8 collective-permute-start
  1686.0 5.1 copy-start
  1686.0 26.7 %all-to-all-start = ((bf16[16,1,128,512]{2,3,1,0:T(8,128)(2,1)}), bf16[16,1,128,512]{2,3,1,0:T(8,128)(2,1)}, u32[]{:S(2)}, u32[]{:S(2)}) async-start(bf16[16,1,128,512]{2,3,1,0:T(8,128)(2,1)} %stack.7), calls=%async_computation | async-start | bytes 4194304 | tf_op jit(solution)/shard_map/while/body/eval_jaxpr/all_to_all | solution.py:106
Sparse Core Ops, SparseCore 0:
  68.9 72.8 all-gather.5
  166.6 157.0 all-gather.5
  348.5 182.3 all-gather.5
  555.6 174.5 all-gather.5
  755.0 177.3 all-gather.5
  957.2 176.3 all-gather.5
  1158.4 182.3 all-gather.5
  1477.2 65.5 all-gather.5
  1679.3 64.4 all-gather.5
